TPU v7x, 32 devices: a whole 2x2x4 slice. The times are simulated.
32 devices in a mesh: rep: 4 (over y, core), fsdp: 4 (over z), seq: 2 (over x).
Axes of the slice: x: 2, y: 2, z: 4, core: 2. Of those that a mesh axis runs over, the one named last changes fastest.
Arguments:
- tokens: bfloat16 [16, 1024, 1024], P(('rep', 'fsdp'), 'seq'), may hold values from -6 to 6
- positions: int32 [3, 16, 1024], P(None, ('rep', 'fsdp'), 'seq'), may hold values from 0 to 15
- input_gain: bfloat16 [1024], P('fsdp'), may hold values from 0.5 to 1.5
- input_shift: bfloat16 [1024], P('fsdp'), may hold values from -1.5 to 1.5
- joint_weight: bfloat16 [1024, 3072], P('fsdp'), may hold values from -0.1875 to 0.1875
- joint_bias: bfloat16 [3072], P('fsdp'), may hold values from -1.5 to 1.5
- output_weight: bfloat16 [1024, 1024], P('fsdp'), may hold values from -3 to 3
- output_bias: bfloat16 [1024], P('fsdp'), may hold values from -1.5 to 1.5
- middle_gain: bfloat16 [1024], P('fsdp'), may hold values from 0.5 to 1.5
- middle_shift: bfloat16 [1024], P('fsdp'), may hold values from -1.5 to 1.5
- expand_weight: bfloat16 [1024, 4096], P('fsdp'), may hold values from -0.1875 to 0.1875
- expand_bias: bfloat16 [4096], P('fsdp'), may hold values from -2.5 to 2.5
- reduce_weight: bfloat16 [4096, 1024], P('fsdp'), may hold values from -0.09375 to 0.09375
- reduce_bias: bfloat16 [1024], P('fsdp'), may hold values from -1.5 to 1.5
- cotangent: bfloat16 [16, 1024, 1024], P(('rep', 'fsdp'), 'seq'), may hold values from -6 to 6
Outputs:
- block_output: bfloat16 [16, 1024, 1024], P(('rep', 'fsdp'), 'seq')
- input_gradient: float32 [16, 1024, 1024], P(('rep', 'fsdp'), 'seq')
- input_gain_gradient: float32 [1024], P('fsdp')
- input_shift_gradient: float32 [1024], P('fsdp')
- joint_weight_gradient: float32 [1024, 3072], P('fsdp')
- joint_bias_gradient: float32 [3072], P('fsdp')
- output_weight_gradient: float32 [1024, 1024], P('fsdp')
- output_bias_gradient: float32 [1024], P('fsdp')
- middle_gain_gradient: float32 [1024], P('fsdp')
- middle_shift_gradient: float32 [1024], P('fsdp')
- expand_weight_gradient: float32 [1024, 4096], P('fsdp')
- expand_bias_gradient: float32 [4096], P('fsdp')
- reduce_weight_gradient: float32 [4096, 1024], P('fsdp')
- reduce_bias_gradient: float32 [1024], P('fsdp')
All inputs are finite; a program needn't handle non-finite values.
Results may differ from a plain program's by a relative error of at most 0.018.
Values may be sent and summed in bfloat16 or wider, within the bound.
No kernel may reach another device: no remote copies, remote signals or barrier semaphores. Data moves between devices by JAX's collectives and lax.ppermute only.
A program may use at most 192 MiB of HBM per device.

v0:
```python
import jax
import jax.numpy as jnp
from jax import lax
from jax.sharding import PartitionSpec as P

epsilon = 1e-06


def norm_rows(values, gains, shifts):
    average = jnp.mean(values, axis=-1, keepdims=True)
    centred = values - average
    spread = jnp.mean(centred * centred, axis=-1, keepdims=True)
    return centred * lax.rsqrt(spread + epsilon) * gains + shifts


def rotary_tables(positions):
    counter = jnp.arange(10).astype(jnp.float32)
    frequency = jnp.power(10000.0, -counter / 10.0)
    angles = positions.astype(jnp.float32)[:, :, None] * frequency
    angles = jnp.transpose(angles, (1, 0, 2))
    return (jnp.cos(angles), jnp.sin(angles))


def rotate(values, cosine_part, sine_part):
    length = values.shape[0]
    heads_count = values.shape[1]
    turned = values[:, :, :60].reshape(length, heads_count, 3, 2, 10)
    former = turned[:, :, :, 0, :]
    latter = turned[:, :, :, 1, :]
    cosine_wide = cosine_part[:, None, :, :]
    sine_wide = sine_part[:, None, :, :]
    new_former = former * cosine_wide - latter * sine_wide
    new_latter = latter * cosine_wide + former * sine_wide
    joined = jnp.stack([new_former, new_latter], axis=3).reshape(length, heads_count, 60)
    return jnp.concatenate([joined, values[:, :, 60:]], axis=2)


def exact_gelu(values):
    return jax.nn.gelu(values, approximate=False)


def split_heads(block):
    return block.reshape(block.shape[0], block.shape[1] // 64, 64)


def group_scores(query_heads, key_heads):
    return (
        jnp.einsum("thd,shd->hts", query_heads, key_heads, preferred_element_type=jnp.float32)
        * 0.125
    )


def attend(inputs):
    query_block, key_block, value_block = inputs
    query_heads = split_heads(query_block)
    key_heads = split_heads(key_block)
    value_heads = split_heads(value_block)
    scores = group_scores(query_heads, key_heads)
    row_max = jnp.max(scores, axis=2, keepdims=True)
    raised = jnp.exp(scores - row_max)
    row_total = jnp.sum(raised, axis=2, keepdims=True)
    probs_low = (raised / row_total).astype(jnp.bfloat16)
    mixed = jnp.einsum("hts,shd->thd", probs_low, value_heads, preferred_element_type=jnp.float32)
    return (mixed.reshape(query_block.shape[0], -1), row_max, row_total)


def attend_back(inputs):
    query_block, key_block, value_block, grad_block, row_max, row_total = inputs
    query_heads = split_heads(query_block)
    key_heads = split_heads(key_block)
    value_heads = split_heads(value_block)
    grad_heads = split_heads(grad_block)
    scores = group_scores(query_heads, key_heads)
    probs = jnp.exp(scores - row_max) / row_total
    probs_low = probs.astype(jnp.bfloat16)
    grad_probs = jnp.einsum(
        "thd,shd->hts", grad_heads, value_heads, preferred_element_type=jnp.float32
    )
    value_grad = jnp.einsum(
        "hts,thd->shd", probs_low, grad_heads, preferred_element_type=jnp.float32
    )
    inner = jnp.sum(grad_probs * probs, axis=2, keepdims=True)
    grad_scores = (probs * (grad_probs - inner)).astype(jnp.bfloat16)
    query_grad = (
        jnp.einsum("hts,shd->thd", grad_scores, key_heads, preferred_element_type=jnp.float32)
        * 0.125
    )
    key_grad = (
        jnp.einsum("hts,thd->shd", grad_scores, query_heads, preferred_element_type=jnp.float32)
        * 0.125
    )
    return (
        query_grad.reshape(query_block.shape[0], -1),
        key_grad.reshape(key_block.shape[0], -1),
        value_grad.reshape(key_block.shape[0], -1),
    )


def local(
    tokens,
    positions,
    input_gain,
    input_shift,
    joint_weight,
    joint_bias,
    output_weight,
    output_bias,
    middle_gain,
    middle_shift,
    expand_weight,
    expand_bias,
    reduce_weight,
    reduce_bias,
    cotangent,
):
    shards = (
        input_gain,
        input_shift,
        joint_weight,
        joint_bias,
        output_weight,
        output_bias,
        middle_gain,
        middle_shift,
        expand_weight,
        expand_bias,
        reduce_weight,
        reduce_bias,
    )
    gathered = (
        lax.all_gather(shards[0], "fsdp", axis=0, tiled=True),
        lax.all_gather(shards[1], "fsdp", axis=0, tiled=True),
        lax.all_gather(shards[2], "fsdp", axis=0, tiled=True),
        lax.all_gather(shards[3], "fsdp", axis=0, tiled=True),
        lax.all_gather(shards[4], "fsdp", axis=0, tiled=True),
        lax.all_gather(shards[5], "fsdp", axis=0, tiled=True),
        lax.all_gather(shards[6], "fsdp", axis=0, tiled=True),
        lax.all_gather(shards[7], "fsdp", axis=0, tiled=True),
        lax.all_gather(shards[8], "fsdp", axis=0, tiled=True),
        lax.all_gather(shards[9], "fsdp", axis=0, tiled=True),
        lax.all_gather(shards[10], "fsdp", axis=0, tiled=True),
        lax.all_gather(shards[11], "fsdp", axis=0, tiled=True),
    )
    row_count = tokens.shape[1]
    width = tokens.shape[2]
    head_count = width // 64
    per_group = min(4, head_count)
    group_count = head_count // per_group
    group_width = per_group * 64

    def to_groups(block):
        return jnp.transpose(block.reshape(block.shape[0], group_count, group_width), (1, 0, 2))

    def from_groups(block):
        return jnp.transpose(block, (1, 0, 2)).reshape(block.shape[1], width)

    residual_in = tokens[0].astype(jnp.float32)
    cosine_part, sine_part = rotary_tables(positions[:, 0, :])
    normed_in = norm_rows(
        residual_in, gathered[0].astype(jnp.float32), gathered[1].astype(jnp.float32)
    ).astype(jnp.bfloat16)
    projected = jnp.dot(normed_in, gathered[2], preferred_element_type=jnp.float32) + gathered[
        3
    ].astype(jnp.float32)
    queries = (
        rotate(projected[:, :width].reshape(row_count, head_count, 64), cosine_part, sine_part)
        .astype(jnp.bfloat16)
        .reshape(row_count, width)
    )
    keys = (
        rotate(
            projected[:, width : 2 * width].reshape(row_count, head_count, 64),
            cosine_part,
            sine_part,
        )
        .astype(jnp.bfloat16)
        .reshape(row_count, width)
    )
    values = projected[:, 2 * width :].astype(jnp.bfloat16)
    query_groups = to_groups(queries)
    key_all, value_all = (
        lax.all_gather(to_groups(keys), "seq", axis=1, tiled=True),
        lax.all_gather(to_groups(values), "seq", axis=1, tiled=True),
    )
    mixed, row_max, row_total = lax.map(attend, (query_groups, key_all, value_all))
    attended = from_groups(mixed).astype(jnp.bfloat16)
    residual_mid = residual_in + (
        jnp.dot(attended, gathered[4], preferred_element_type=jnp.float32)
        + gathered[5].astype(jnp.float32)
    )
    normed_mid = norm_rows(
        residual_mid, gathered[6].astype(jnp.float32), gathered[7].astype(jnp.float32)
    ).astype(jnp.bfloat16)
    upper = jnp.dot(normed_mid, gathered[8], preferred_element_type=jnp.float32) + gathered[
        9
    ].astype(jnp.float32)
    hidden = exact_gelu(upper).astype(jnp.bfloat16)
    result = residual_mid + (
        jnp.dot(hidden, gathered[10], preferred_element_type=jnp.float32)
        + gathered[11].astype(jnp.float32)
    )
    block_output = result.astype(jnp.bfloat16)[None]
    again = (
        lax.all_gather(shards[0], "fsdp", axis=0, tiled=True),
        lax.all_gather(shards[1], "fsdp", axis=0, tiled=True),
        lax.all_gather(shards[2], "fsdp", axis=0, tiled=True),
        lax.all_gather(shards[3], "fsdp", axis=0, tiled=True),
        lax.all_gather(shards[4], "fsdp", axis=0, tiled=True),
        lax.all_gather(shards[5], "fsdp", axis=0, tiled=True),
        lax.all_gather(shards[6], "fsdp", axis=0, tiled=True),
        lax.all_gather(shards[7], "fsdp", axis=0, tiled=True),
        lax.all_gather(shards[8], "fsdp", axis=0, tiled=True),
        lax.all_gather(shards[9], "fsdp", axis=0, tiled=True),
        lax.all_gather(shards[10], "fsdp", axis=0, tiled=True),
        lax.all_gather(shards[11], "fsdp", axis=0, tiled=True),
    )
    grad_low = cotangent[0]
    grad_out = grad_low.astype(jnp.float32)
    reduce_term = jnp.einsum("tf,td->fd", hidden, grad_low, preferred_element_type=jnp.float32)
    reduce_offset_term = jnp.sum(grad_out, axis=0)
    grad_hidden = jnp.einsum("td,fd->tf", grad_low, again[10], preferred_element_type=jnp.float32)
    gelu_pull = jax.vjp(exact_gelu, upper)[1]
    grad_upper = gelu_pull(grad_hidden)[0].astype(jnp.bfloat16)
    expand_term = jnp.einsum(
        "td,tf->df", normed_mid, grad_upper, preferred_element_type=jnp.float32
    )
    expand_offset_term = jnp.sum(grad_upper.astype(jnp.float32), axis=0)
    grad_mid_norm = jnp.einsum(
        "tf,df->td", grad_upper, again[8], preferred_element_type=jnp.float32
    )
    middle_pull = jax.vjp(
        norm_rows, residual_mid, again[6].astype(jnp.float32), again[7].astype(jnp.float32)
    )[1]
    grad_mid_in, middle_gain_term, middle_shift_term = middle_pull(grad_mid_norm)
    grad_resid = grad_out + grad_mid_in
    grad_branch = grad_resid.astype(jnp.bfloat16)
    output_term = jnp.einsum("td,te->de", attended, grad_branch, preferred_element_type=jnp.float32)
    output_offset_term = jnp.sum(grad_branch.astype(jnp.float32), axis=0)
    grad_attended = jnp.einsum(
        "te,de->td", grad_branch, again[4], preferred_element_type=jnp.float32
    ).astype(jnp.bfloat16)
    query_grad, key_grad, value_grad = lax.map(
        attend_back,
        (query_groups, key_all, value_all, to_groups(grad_attended), row_max, row_total),
    )
    key_share, value_share = (
        lax.psum_scatter(
            key_grad.astype(jnp.bfloat16), "seq", scatter_dimension=1, tiled=True
        ).astype(jnp.float32),
        lax.psum_scatter(
            value_grad.astype(jnp.bfloat16), "seq", scatter_dimension=1, tiled=True
        ).astype(jnp.float32),
    )
    grad_query = rotate(
        from_groups(query_grad).reshape(row_count, head_count, 64), cosine_part, -sine_part
    ).reshape(row_count, width)
    grad_key = rotate(
        from_groups(key_share).reshape(row_count, head_count, 64), cosine_part, -sine_part
    ).reshape(row_count, width)
    grad_value = from_groups(value_share)
    grad_projected = jnp.concatenate([grad_query, grad_key, grad_value], axis=1).astype(
        jnp.bfloat16
    )
    joint_term = jnp.einsum(
        "td,te->de", normed_in, grad_projected, preferred_element_type=jnp.float32
    )
    joint_offset_term = jnp.sum(grad_projected.astype(jnp.float32), axis=0)
    grad_in_norm = jnp.einsum(
        "te,de->td", grad_projected, again[2], preferred_element_type=jnp.float32
    )
    input_pull = jax.vjp(
        norm_rows, residual_in, again[0].astype(jnp.float32), again[1].astype(jnp.float32)
    )[1]
    grad_first_in, input_gain_term, input_shift_term = input_pull(grad_in_norm)
    input_gradient = (grad_resid + grad_first_in)[None]
    terms = (
        input_gain_term,
        input_shift_term,
        joint_term,
        joint_offset_term,
        output_term,
        output_offset_term,
        middle_gain_term,
        middle_shift_term,
        expand_term,
        expand_offset_term,
        reduce_term,
        reduce_offset_term,
    )
    owned = (
        lax.psum_scatter(
            terms[0].astype(jnp.bfloat16), "fsdp", scatter_dimension=0, tiled=True
        ).astype(jnp.float32),
        lax.psum_scatter(
            terms[1].astype(jnp.bfloat16), "fsdp", scatter_dimension=0, tiled=True
        ).astype(jnp.float32),
        lax.psum_scatter(
            terms[2].astype(jnp.bfloat16), "fsdp", scatter_dimension=0, tiled=True
        ).astype(jnp.float32),
        lax.psum_scatter(
            terms[3].astype(jnp.bfloat16), "fsdp", scatter_dimension=0, tiled=True
        ).astype(jnp.float32),
        lax.psum_scatter(
            terms[4].astype(jnp.bfloat16), "fsdp", scatter_dimension=0, tiled=True
        ).astype(jnp.float32),
        lax.psum_scatter(
            terms[5].astype(jnp.bfloat16), "fsdp", scatter_dimension=0, tiled=True
        ).astype(jnp.float32),
        lax.psum_scatter(
            terms[6].astype(jnp.bfloat16), "fsdp", scatter_dimension=0, tiled=True
        ).astype(jnp.float32),
        lax.psum_scatter(
            terms[7].astype(jnp.bfloat16), "fsdp", scatter_dimension=0, tiled=True
        ).astype(jnp.float32),
        lax.psum_scatter(
            terms[8].astype(jnp.bfloat16), "fsdp", scatter_dimension=0, tiled=True
        ).astype(jnp.float32),
        lax.psum_scatter(
            terms[9].astype(jnp.bfloat16), "fsdp", scatter_dimension=0, tiled=True
        ).astype(jnp.float32),
        lax.psum_scatter(
            terms[10].astype(jnp.bfloat16), "fsdp", scatter_dimension=0, tiled=True
        ).astype(jnp.float32),
        lax.psum_scatter(
            terms[11].astype(jnp.bfloat16), "fsdp", scatter_dimension=0, tiled=True
        ).astype(jnp.float32),
    )
    summed = (
        lax.psum(owned[0].astype(jnp.bfloat16), ("rep", "seq")).astype(jnp.float32),
        lax.psum(owned[1].astype(jnp.bfloat16), ("rep", "seq")).astype(jnp.float32),
        lax.psum(owned[2].astype(jnp.bfloat16), ("rep", "seq")).astype(jnp.float32),
        lax.psum(owned[3].astype(jnp.bfloat16), ("rep", "seq")).astype(jnp.float32),
        lax.psum(owned[4].astype(jnp.bfloat16), ("rep", "seq")).astype(jnp.float32),
        lax.psum(owned[5].astype(jnp.bfloat16), ("rep", "seq")).astype(jnp.float32),
        lax.psum(owned[6].astype(jnp.bfloat16), ("rep", "seq")).astype(jnp.float32),
        lax.psum(owned[7].astype(jnp.bfloat16), ("rep", "seq")).astype(jnp.float32),
        lax.psum(owned[8].astype(jnp.bfloat16), ("rep", "seq")).astype(jnp.float32),
        lax.psum(owned[9].astype(jnp.bfloat16), ("rep", "seq")).astype(jnp.float32),
        lax.psum(owned[10].astype(jnp.bfloat16), ("rep", "seq")).astype(jnp.float32),
        lax.psum(owned[11].astype(jnp.bfloat16), ("rep", "seq")).astype(jnp.float32),
    )
    return (
        block_output,
        input_gradient,
        summed[0],
        summed[1],
        summed[2],
        summed[3],
        summed[4],
        summed[5],
        summed[6],
        summed[7],
        summed[8],
        summed[9],
        summed[10],
        summed[11],
    )


def solution(mesh):
    return jax.shard_map(
        local,
        mesh=mesh,
        in_specs=(
            P(("rep", "fsdp"), "seq", None),
            P(None, ("rep", "fsdp"), "seq"),
            P("fsdp"),
            P("fsdp"),
            P("fsdp", None),
            P("fsdp"),
            P("fsdp", None),
            P("fsdp"),
            P("fsdp"),
            P("fsdp"),
            P("fsdp", None),
            P("fsdp"),
            P("fsdp", None),
            P("fsdp"),
            P(("rep", "fsdp"), "seq", None),
        ),
        out_specs=(
            P(("rep", "fsdp"), "seq", None),
            P(("rep", "fsdp"), "seq", None),
            P("fsdp"),
            P("fsdp"),
            P("fsdp", None),
            P("fsdp"),
            P("fsdp", None),
            P("fsdp"),
            P("fsdp"),
            P("fsdp"),
            P("fsdp", None),
            P("fsdp"),
            P("fsdp", None),
            P("fsdp"),
        ),
        check_vma=False,
    )
```

profile of v0, /device:TPU:0, one launch (start us, length us, event | category | flops | bytes accessed | tf_op | source)
XLA Modules:
  0.0 1273.0 jit_solution(16139119386478265900)
XLA Ops:
  8.6 14.8 %all-gather.2 = bf16[4,1,768]{2,1,0:T(2,128)(2,1)S(1)} all-gather(bf16[1,1,768]{2,1,0:T(2,128)(2,1)S(1)} %reshape.244), channel_id=1, replica_groups=mesh['rep'=4,'fsdp'=4,'seq'=2] {'fsdp'}, dimensions={0}, use_global_device_ids=true | all-gather | bytes 7680 | tf_op jit(solution)/shard_map/all_gather | solution.py:134
  24.2 12.4 all-gather.1
  49.0 78.8 %all-gather.14.cloned.1.call-done = bf16[1024,3072]{1,0:T(8,128)(2,1)} async-done(((bf16[256,3072]{1,0:T(8,128)(2,1)}), bf16[1024,3072]{1,0:T(8,128)(2,1)}) %all-gather.14.cloned.1.call-update) | async-done | bytes 6291472 | tf_op jit(solution)/shard_map/all_gather | solution.py:133
  167.4 11.9 all_gather.59
  187.7 9.1 all-gather.4
  204.7 31.5 %while.30 = (s32[]{:T(128)}, bf16[4,512,256]{1,2,0:T(8,128)(2,1)S(1)}, f32[4,4,512,1]{2,1,3,0:T(4,128)S(1)}, f32[4,4,512,1]{2,1,3,0:T(4,128)S(1)}, bf16[4,1024,2...) while((s32[]{:T(128)}, ...), condition=%wide.region_5.6_spmd.clone, body=%wide.region_2.5_spmd.sunk.clone | while | flops 555741184 | bytes 29958248 | solution.py:185
  236.2 15.6 %all-gather.20.cloned.1.call-done = bf16[1024,1024]{1,0:T(8,128)(2,1)} async-done(((bf16[256,1024]{1,0:T(8,128)(2,1)}), bf16[1024,1024]{1,0:T(8,128)(2,1)}) %all-gather.20.cloned.1.call-update) | async-done | bytes 2097168 | tf_op jit(solution)/shard_map/all_gather | solution.py:135
  255.5 146.2 %all-gather.22.cloned.1.call-done = bf16[1024,4096]{1,0:T(8,128)(2,1)} async-done(((bf16[256,4096]{1,0:T(8,128)(2,1)}), bf16[1024,4096]{1,0:T(8,128)(2,1)}) %all-gather.22.cloned.1.call-update) | async-done | bytes 8388624 | tf_op jit(solution)/shard_map/all_gather | solution.py:139
  401.7 27.6 %multiply_convert_fusion.1 = (bf16[512,4096]{1,0:T(8,128)(2,1)}, f32[512,4096]{1,0:T(8,128)}, f32[512,4096]{1,0:T(8,128)}) fusion(f32[4096]{0:T(1024)S(1)} %convert_element_type.220, bf16[1024,4096]{1,0:T(8,128)(2,1)} %all-gather.22.cloned.1.call-done, f32[512,1024]{1,0:T(8,128)S(1)} %get-tuple-element.210, f32[1024]{0:T(1024)S(1)} %bitcast.295, ...), kind=kOutput, calls=%fused_computation.31 | convolution fusion | flops 4436000768 | bytes 31485952 | tf_op jit(solution)/shard_map/dot_general | solution.py:194
  429.3 121.7 %all-gather.24.cloned.1.call-done = bf16[4096,1024]{1,0:T(8,128)(2,1)} async-done(((bf16[1024,1024]{1,0:T(8,128)(2,1)}), bf16[4096,1024]{1,0:T(8,128)(2,1)}) %all-gather.24.cloned.1.call-update) | async-done | bytes 8388624 | tf_op jit(solution)/shard_map/all_gather | solution.py:141
  550.9 15.9 %fusion.47 = (bf16[4096]{0:T(1024)(128)(2,1)}, bf16[512,4096]{1,0:T(8,128)(2,1)}) fusion(f32[512,4096]{1,0:T(8,128)} %get-tuple-element.179, bf16[4096,1024]{1,0:T(8,128)(2,1)} %all-gather.24.cloned.1.call-done, bf16[1,512,1024]{2,1,0:T(8,128)(2,1)S(1)} %copy-done.7, f32[512,4096]{1,0:T(8,128)} %get-tuple-element.211, f32[4096]{0:T(1024)S(1)} %convert_element_type.220), kind=kOutput, calls=%fused_computation.125 | convolution fusion | flops 4328517632 | bytes 30433280 | tf_op jit(solution)/shard_map/td,fd->tf/dot_general | solution.py:221
  582.3 47.7 %while.31 = (s32[]{:T(128)}, f32[4,512,256]{1,2,0:T(8,128)S(1)}, bf16[4,1024,256]{1,2,0:T(8,128)(2,1)}, bf16[4,1024,256]{1,2,0:T(8,128)(2,1)}, bf16[4,1024,256]{...) while((s32[]{:T(128)}, f32[4,512,256]{1,2,0:T(8,128)S(1)}, ...), condition=%wide.region_12.13_spmd.clone, body=%wide.region_10.12_spmd.sunk.clone | while | flops 1361704960 | bytes 73465992 | solution.py:242
  639.0 21.3 %reduce-scatter.7.cloned.1.call-done = bf16[4,512,256]{1,2,0:T(8,128)(2,1)} async-done(((bf16[4,1024,256]{1,2,0:T(8,128)(2,1)}), bf16[4,512,256]{1,2,0:T(8,128)(2,1)}) %reduce-scatter.7.cloned.1.call-update) | async-done | bytes 1048592 | tf_op jit(solution)/shard_map/reduce_scatter | solution.py:247
  665.8 28.7 %reduce-scatter.9.cloned.1.call-done = bf16[4,512,256]{1,2,0:T(8,128)(2,1)} async-done(((bf16[4,1024,256]{1,2,0:T(8,128)(2,1)}), bf16[4,512,256]{1,2,0:T(8,128)(2,1)}) %reduce-scatter.9.cloned.1.call-update) | async-done | bytes 1048592 | tf_op jit(solution)/shard_map/reduce_scatter | solution.py:250
  704.0 9.2 convolution_convert_fusion.1
  713.5 10.4 convolution_convert_fusion
  724.5 11.5 all-gather.6
  740.5 112.2 %reduce-scatter.11.cloned.1.call-done = bf16[256,3072]{1,0:T(8,128)(2,1)} async-done(((bf16[1024,3072]{1,0:T(8,128)(2,1)}), bf16[256,3072]{1,0:T(8,128)(2,1)}) %reduce-scatter.11.cloned.1.call-update) | async-done | bytes 1572880 | tf_op jit(solution)/shard_map/reduce_scatter | solution.py:297
  852.7 147.5 %reduce-scatter.15.cloned.1.call-done = bf16[256,4096]{1,0:T(8,128)(2,1)} async-done(((bf16[1024,4096]{1,0:T(8,128)(2,1)}), bf16[256,4096]{1,0:T(8,128)(2,1)}) %reduce-scatter.15.cloned.1.call-update) | async-done | bytes 2097168 | tf_op jit(solution)/shard_map/reduce_scatter | solution.py:315
  1000.1 147.5 %reduce-scatter.17.cloned.1.call-done = bf16[1024,1024]{1,0:T(8,128)(2,1)} async-done(((bf16[4096,1024]{1,0:T(8,128)(2,1)}), bf16[1024,1024]{1,0:T(8,128)(2,1)}) %reduce-scatter.17.cloned.1.call-update) | async-done | bytes 2097168 | tf_op jit(solution)/shard_map/reduce_scatter | solution.py:321
  1147.7 10.3 fusion.24
  1167.2 18.9 %all-reduce.10 = (bf16[1024]{0:T(1024)(128)(2,1)S(1)}, bf16[1024]{0:T(1024)(128)(2,1)S(1)}, bf16[3072]{0:T(1024)(128)(2,1)S(1)}, bf16[1024]{0:T(1024)(128)(2,1)S...) all-reduce(bf16[1024]{0:T(1024)(128)(2,1)S(1)} %get-tuple-element.1, ...), channel_id=4, replica_groups=mesh['rep'=4,'fsdp'=4,'seq'=2] {'fsdp'}, use_global_device_ids=true, to_apply=%region_18.19.clone | all-reduce | flops 13312 | bytes 53248
  1186.6 14.8 %all-reduce.8 = (bf16[256]{0:T(256)(128)(2,1)S(1)}, bf16[256]{0:T(256)(128)(2,1)S(1)}, bf16[768]{0:T(1024)(128)(2,1)S(1)}, bf16[256]{0:T(256)(128)(2,1)S(1)}, bf...) all-reduce(bf16[256]{0:T(256)(128)(2,1)S(1)} %dynamic-slice.1, ...), channel_id=1, replica_groups=mesh['rep'=4,'fsdp'=4,'seq'=2] {'rep','seq'}, use_global_device_ids=true, to_apply=%region_19.20 | all-reduce | flops 3328 | bytes 13312 | tf_op jit(solution)/shard_map/psum | solution.py:329
  1210.2 46.2 %all-reduce.13.cloned.1.call-done = (bf16[256,3072]{1,0:T(8,128)(2,1)}, bf16[256,1024]{1,0:T(8,128)(2,1)}, bf16[256,4096]{1,0:T(8,128)(2,1)}, bf16[1024,1024]{1,0:T(8,128)(2,1)}) async-done(((bf16[256,3072]{1,0:T(8,128)(2,1)}, bf16[256,1024]{1,0:T(8,128)(2,1)}, bf16[256,4096]{1,0:T(8,128)(2,1)}, bf16[1024,1024]{1,0:T(8,128)(2,1)}), (bf16[256,3072]{1,0:T(8,128)(2,1)}, bf16[256,1024]{1,0:T(8,128)(2,1)}, ...) | async-done | bytes 6291472 | tf_op jit(solution)/shard_map/psum | solution.py:331
  (332 shorter events, 223.1 us)
Async XLA Ops:
  7.2 120.6 %all-gather.14.cloned.1.call-start = ((), (), s32[]{:S(2)}) async-start(), calls=%async_computation.6 | async-start | bytes 7864320 | tf_op jit(solution)/shard_map/all_gather | solution.py:133
  7.9 190.9 %all-gather.16.cloned.1.call-start = ((), (), s32[]{:S(2)}) async-start(), calls=%async_computation.7 | async-start | bytes 3145728 | tf_op jit(solution)/shard_map/all_gather | solution.py:183
  36.6 91.2 %copy-start.46 = (f32[4,1,256]{2,1,0:T(1,128)}, f32[4,1,256]{2,1,0:T(1,128)S(1)}, u32[]{:S(2)}) copy-start(f32[4,1,256]{2,1,0:T(1,128)S(1)} %convert_element_type.251) | copy-start | bytes 12292
  45.3 82.5 %copy-start.27 = (f32[4,1,256]{2,1,0:T(1,128)}, f32[4,1,256]{2,1,0:T(1,128)S(1)}, u32[]{:S(2)}) copy-start(f32[4,1,256]{2,1,0:T(1,128)S(1)} %convert_element_type.250) | copy-start | bytes 12292
  46.7 81.0 %copy-start.29 = (f32[512]{0:T(512)}, f32[512]{0:T(512)S(1)}, u32[]{:S(2)}) copy-start(f32[512]{0:T(512)S(1)} %broadcast_multiply_fusion.1) | copy-start | bytes 6148
  49.0 78.8 %copy-start.35 = (f32[512]{0:T(512)}, f32[512]{0:T(512)S(1)}, u32[]{:S(2)}) copy-start(f32[512]{0:T(512)S(1)} %fusion.32) | copy-start | bytes 6148
  138.0 66.7 %all-gather.18.cloned.1.call-start = ((), (), s32[]{:S(2)}) async-start(), calls=%async_computation.8 | async-start | bytes 3145728 | tf_op jit(solution)/shard_map/all_gather | solution.py:182
  157.5 94.3 %all-gather.20.cloned.1.call-start = ((), (), s32[]{:S(2)}) async-start(), calls=%async_computation.9 | async-start | bytes 2621440 | tf_op jit(solution)/shard_map/all_gather | solution.py:135
  158.1 243.6 %all-gather.22.cloned.1.call-start = ((), (), s32[]{:S(2)}) async-start(), calls=%async_computation.10 | async-start | bytes 10485760 | tf_op jit(solution)/shard_map/all_gather | solution.py:139
  158.7 392.3 %all-gather.24.cloned.1.call-start = ((), (), s32[]{:S(2)}) async-start(), calls=%async_computation.11 | async-start | bytes 10485760 | tf_op jit(solution)/shard_map/all_gather | solution.py:141
  159.3 501.0 %reduce-scatter.7.cloned.1.call-start = ((), (), s32[]{:S(2)}) async-start(), calls=%async_computation.12 | async-start | bytes 3145728 | tf_op jit(solution)/shard_map/reduce_scatter | solution.py:247
  187.7 214.0 %copy-start.48 = (f32[4,1,256]{2,1,0:T(1,128)}, f32[4,1,256]{2,1,0:T(1,128)S(1)}, u32[]{:S(2)}) copy-start(f32[4,1,256]{2,1,0:T(1,128)S(1)} %convert_element_type.255) | copy-start | bytes 12292
  196.8 377.6 %copy-start.39 = (f32[4,1,256]{2,1,0:T(1,128)}, f32[4,1,256]{2,1,0:T(1,128)S(1)}, u32[]{:S(2)}) copy-start(f32[4,1,256]{2,1,0:T(1,128)S(1)} %convert_element_type.254) | copy-start | bytes 12292
  204.7 47.1 %copy-start = (bf16[1,512,1024]{2,1,0:T(8,128)(2,1)S(1)}, bf16[1,512,1024]{2,1,0:T(8,128)(2,1)}, u32[]{:S(2)}) copy-start(bf16[1,512,1024]{2,1,0:T(8,128)(2,1)} %param.19) | copy-start | bytes 3145732
  255.1 319.3 %copy-start.4 = (f32[512,1024]{1,0:T(8,128)}, f32[512,1024]{1,0:T(8,128)S(1)}, u32[]{:S(2)}) copy-start(f32[512,1024]{1,0:T(8,128)S(1)} %get-tuple-element.210) | copy-start | bytes 6291460
  255.1 319.3 %copy-start.37 = (f32[512]{0:T(512)}, f32[512]{0:T(512)S(1)}, u32[]{:S(2)}) copy-start(f32[512]{0:T(512)S(1)} %broadcast_multiply_fusion) | copy-start | bytes 6148
  255.5 319.0 %copy-start.42 = (f32[512]{0:T(512)}, f32[512]{0:T(512)S(1)}, u32[]{:S(2)}) copy-start(f32[512]{0:T(512)S(1)} %fusion.33) | copy-start | bytes 6148
  401.7 149.3 %copy-start.7 = (bf16[1,512,1024]{2,1,0:T(8,128)(2,1)S(1)}, bf16[1,512,1024]{2,1,0:T(8,128)(2,1)}, u32[]{:S(2)}) copy-start(bf16[1,512,1024]{2,1,0:T(8,128)(2,1)} %param.33) | copy-start | bytes 3145732
  630.1 64.4 %reduce-scatter.9.cloned.1.call-start = ((), (), s32[]{:S(2)}) async-start(), calls=%async_computation.13 | async-start | bytes 3145728 | tf_op jit(solution)/shard_map/reduce_scatter | solution.py:250
  630.8 109.7 %reduce-scatter.13.cloned.1.call-start = ((), (), s32[]{:S(2)}) async-start(), calls=%async_computation.15 | async-start | bytes 2621440 | tf_op jit(solution)/shard_map/reduce_scatter | solution.py:303
  635.9 216.8 %reduce-scatter.11.cloned.1.call-start = ((), (), s32[]{:S(2)}) async-start(), calls=%async_computation.14 | async-start | bytes 7864320 | tf_op jit(solution)/shard_map/reduce_scatter | solution.py:297
  702.3 297.9 %reduce-scatter.15.cloned.1.call-start = ((), (), s32[]{:S(2)}) async-start(), calls=%async_computation.16 | async-start | bytes 10485760 | tf_op jit(solution)/shard_map/reduce_scatter | solution.py:315
  713.2 434.4 %reduce-scatter.17.cloned.1.call-start = ((), (), s32[]{:S(2)}) async-start(), calls=%async_computation.17 | async-start | bytes 10485760 | tf_op jit(solution)/shard_map/reduce_scatter | solution.py:321
  723.9 532.5 %all-reduce.13.cloned.1.call-start = ((), (), s32[]{:S(2)}) async-start(), calls=%async_computation.18 | async-start | bytes 12582912 | tf_op jit(solution)/shard_map/psum | solution.py:331
  (48 other events, 586.4 us)
Sparse Core Ops, SparseCore 0:
  9.6 118.1 all-gather.13
  138.1 31.2 all-gather.15
  171.6 33.0 all-gather.17
  206.1 45.6 all-gather.19
  253.2 148.4 all-gather.21
  403.1 147.7 all-gather.23
  630.2 30.0 reduce-scatter.6
  662.5 31.8 reduce-scatter.8
  696.8 43.6 reduce-scatter.12
  742.6 109.9 reduce-scatter.10
  855.0 145.0 reduce-scatter.14
  1002.3 145.2 reduce-scatter.16
  1151.2 105.1 all-reduce.12
where the time goes:
time: 1280 us; the launch traced here: 1270 us
  waiting for transfers between devices  875 us (68%)
  matrix products  154 us (12%)
  blocking collectives  118 us (9%)
  local copies, waits for them, and re-layouts  64 us (5%)
  other arithmetic  43.8 us (3%)
  between operations  17.1 us (1%)
    reduce_scatter x1, waiting for transfers between devices, local(): lax.psum_scatter(terms[8].astype(jnp.bfloat16), 'fsdp', scatter_dimension...  147 us
    reduce_scatter x1, waiting for transfers between devices, local(): lax.psum_scatter(terms[10].astype(jnp.bfloat16), 'fsdp', scatter_dimensio...  147 us
    all_gather x1, waiting for transfers between devices, local(): lax.all_gather(shards[8], 'fsdp', axis=0, tiled=True)  146 us
    all_gather x1, waiting for transfers between devices, local(): lax.all_gather(shards[10], 'fsdp', axis=0, tiled=True)  122 us
    reduce_scatter x1, waiting for transfers between devices, local(): lax.psum_scatter(terms[2].astype(jnp.bfloat16), 'fsdp', scatter_dimension...  112 us
    all_gather x1, waiting for transfers between devices, local(): lax.all_gather(shards[2], 'fsdp', axis=0, tiled=True)  78.8 us
    psum x1, waiting for transfers between devices, local(): lax.psum(owned[2].astype(jnp.bfloat16), ('rep', 'seq')).astype(jnp.float32)  46.2 us
    reduce_scatter x1, waiting for transfers between devices, local(): lax.psum_scatter(value_grad.astype(jnp.bfloat16), 'seq', scatter_dimensio...  28.7 us
  transfers between devices with their start and end apart: 13, of which 12 were waited for; matrix products, arithmetic and copies ran while one was open for 12% of the time, Pallas kernels for 0%

commit v1 on v0

--- a/solution.py
+++ b/solution.py
@@ -4,6 +4,24 @@
 from jax.sharding import PartitionSpec as P
 
 epsilon = 1e-06
+
+
+def gather_around(array, axis, dim):
+    ways, here, step = (lax.axis_size(axis), lax.axis_index(axis), array.shape[dim])
+    shape = [n * ways if d == dim else n for d, n in enumerate(array.shape)]
+    full = lax.dynamic_update_slice_in_dim(
+        jnp.zeros(shape, array.dtype), array, here * step, axis=dim
+    )
+    going_up = going_down = array
+    for far in range(1, ways // 2 + 1):
+        going_up = lax.ppermute(going_up, axis, [(d, (d + 1) % ways) for d in range(ways)])
+        full = lax.dynamic_update_slice_in_dim(full, going_up, (here - far) % ways * step, axis=dim)
+        if 2 * far < ways:
+            going_down = lax.ppermute(going_down, axis, [(d, (d - 1) % ways) for d in range(ways)])
+            full = lax.dynamic_update_slice_in_dim(
+                full, going_down, (here + far) % ways * step, axis=dim
+            )
+    return full
 
 
 def norm_rows(values, gains, shifts):
@@ -136,7 +154,7 @@
         lax.all_gather(shards[5], "fsdp", axis=0, tiled=True),
         lax.all_gather(shards[6], "fsdp", axis=0, tiled=True),
         lax.all_gather(shards[7], "fsdp", axis=0, tiled=True),
-        lax.all_gather(shards[8], "fsdp", axis=0, tiled=True),
+        gather_around(shards[8], "fsdp", 0),
         lax.all_gather(shards[9], "fsdp", axis=0, tiled=True),
         lax.all_gather(shards[10], "fsdp", axis=0, tiled=True),
         lax.all_gather(shards[11], "fsdp", axis=0, tiled=True),

time: 1280 us -> 1340 us (1.047)
  blocking collectives: 118 us -> 273 us
  waiting for transfers between devices: 875 us -> 758 us
  local copies, waits for them, and re-layouts: 64 us -> 78.4 us
    all_gather x1, blocking collectives: 7.97 us -> 151 us  [local(): lax.all_gather(shards[5], 'fsdp', axis=0, tiled=True)]
    all_gather x1, waiting for transfers between devices: 122 us -> 0.01 us  [local(): lax.all_gather(shards[10], 'fsdp', axis=0, tiled=True)]
    ppermute x0 -> x3, waiting for transfers between devices: none -> 46.8 us  [the longest x2 46.8 us: gather_around(): lax.ppermute(going_up, axis, [(d, (d + 1) % ways) for d in range(ways)])]
    all_gather x1, waiting for transfers between devices: 146 us -> 123 us  [local(): lax.all_gather(shards[8], 'fsdp', axis=0, tiled=True)]
    all_gather x1, waiting for transfers between devices: 15.6 us -> 0.02 us  [local(): lax.all_gather(shards[4], 'fsdp', axis=0, tiled=True)]
  transfers between devices with their start and end apart: 13 -> 16, of which waited for: 12 -> 10; matrix products, arithmetic and copies ran while one was open for 12% -> 13% of each run, Pallas kernels for 0% -> 0%
where the time goes in v1:
time: 1340 us; the launch traced here: 1330 us
  waiting for transfers between devices  758 us (57%)
  blocking collectives  273 us (20%)
  matrix products  153 us (11%)
  local copies, waits for them, and re-layouts  78.4 us (6%)
  other arithmetic  42.6 us (3%)
  between operations  17.3 us (1%)
    all_gather x1, blocking collectives, local(): lax.all_gather(shards[5], 'fsdp', axis=0, tiled=True)  151 us
    reduce_scatter x1, waiting for transfers between devices, local(): lax.psum_scatter(terms[8].astype(jnp.bfloat16), 'fsdp', scatter_dimension...  147 us
    reduce_scatter x1, waiting for transfers between devices, local(): lax.psum_scatter(terms[10].astype(jnp.bfloat16), 'fsdp', scatter_dimensio...  146 us
    all_gather x1, waiting for transfers between devices, local(): lax.all_gather(shards[8], 'fsdp', axis=0, tiled=True)  123 us
    reduce_scatter x1, waiting for transfers between devices, local(): lax.psum_scatter(terms[2].astype(jnp.bfloat16), 'fsdp', scatter_dimension...  114 us
    all_gather x1, waiting for transfers between devices, local(): lax.all_gather(shards[2], 'fsdp', axis=0, tiled=True)  78.8 us
    ppermute x2, waiting for transfers between devices, gather_around(): lax.ppermute(going_up, axis, [(d, (d + 1) % ways) for d in range(ways)])  46.8 us
    psum x1, waiting for transfers between devices, local(): lax.psum(owned[2].astype(jnp.bfloat16), ('rep', 'seq')).astype(jnp.float32)  46.2 us
  transfers between devices with their start and end apart: 16, of which 10 were waited for; matrix products, arithmetic and copies ran while one was open for 13% of the time, Pallas kernels for 0%

profile of v1, /device:TPU:0, one launch (start us, length us, event | category | flops | bytes accessed | tf_op | source)
XLA Modules:
  0.0 1327.5 jit_solution(15498730047374321025)
XLA Ops:
  8.6 14.8 %all-gather.2 = bf16[4,1,768]{2,1,0:T(2,128)(2,1)S(1)} all-gather(bf16[1,1,768]{2,1,0:T(2,128)(2,1)S(1)} %reshape.244), channel_id=1, replica_groups=mesh['rep'=4,'fsdp'=4,'seq'=2] {'fsdp'}, dimensions={0}, use_global_device_ids=true | all-gather | bytes 7680 | tf_op jit(solution)/shard_map/all_gather | solution.py:152
  24.2 12.4 all-gather.1
  49.0 78.8 %all-gather.14.cloned.1.call-done = bf16[1024,3072]{1,0:T(8,128)(2,1)} async-done(((bf16[256,3072]{1,0:T(8,128)(2,1)}), bf16[1024,3072]{1,0:T(8,128)(2,1)}) %all-gather.14.cloned.1.call-update) | async-done | bytes 6291472 | tf_op jit(solution)/shard_map/all_gather | solution.py:151
  162.6 46.8 %collective-permute-done = bf16[256,4096]{1,0:T(8,128)(2,1)} collective-permute-done((bf16[256,4096]{1,0:T(8,128)(2,1)}, bf16[256,4096]{1,0:T(8,128)(2,1)}, u32[]{:S(2)}, u32[]{:S(2)}) %collective-permute-start) | collective-permute-done | bytes 2097184 | tf_op jit(solution)/shard_map/ppermute | solution.py:17
  209.7 151.1 %all-gather.3 = bf16[4,1,256]{2,1,0:T(2,128)(2,1)S(1)} all-gather(bf16[1,1,256]{2,1,0:T(2,128)(2,1)S(1)} %reshape.246), channel_id=1, replica_groups=mesh['rep'=4,'fsdp'=4,'seq'=2] {'fsdp'}, dimensions={0}, use_global_device_ids=true | all-gather | bytes 2560 | tf_op jit(solution)/shard_map/all_gather | solution.py:154
  360.8 18.8 %all_gather.57 = bf16[4096]{0:T(1024)(128)(2,1)S(1)} all-gather(bf16[1024]{0:T(1024)(128)(2,1)S(1)} %copy-done.51), channel_id=1, replica_groups=mesh['rep'=4,'fsdp'=4,'seq'=2] {'fsdp'}, dimensions={0}, use_global_device_ids=true | all-gather | bytes 10240 | tf_op jit(solution)/shard_map/all_gather | solution.py:158
  379.6 11.3 all-gather.5
  390.9 11.3 all-gather.4
  414.0 31.6 %while.30 = (s32[]{:T(128)}, bf16[4,512,256]{1,2,0:T(8,128)(2,1)S(1)}, f32[4,4,512,1]{2,1,3,0:T(4,128)S(1)}, f32[4,4,512,1]{2,1,3,0:T(4,128)S(1)}, bf16[4,1024,2...) while((s32[]{:T(128)}, ...), condition=%wide.region_5.6_spmd.clone, body=%wide.region_2.5_spmd.sunk.clone | while | flops 555741184 | bytes 29958248 | solution.py:203
  451.3 26.3 %multiply_convert_fusion.1 = (bf16[512,4096]{1,0:T(8,128)(2,1)}, f32[512,4096]{1,0:T(8,128)}, f32[512,4096]{1,0:T(8,128)}) fusion(f32[4096]{0:T(1024)S(1)} %convert_element_type.220, bf16[1024,4096]{1,0:T(8,128)(2,1)S(1)} %copy-done.10, f32[512,1024]{1,0:T(8,128)S(1)} %get-tuple-element.210, f32[1024]{0:T(1024)S(1)} %bitcast.295, f32[1024]{0:T(1024)S(1)} %bitcast.288, ...), kind=kOutput, calls=%fused_computation.31 | convolution fusion | flops 4436000768 | bytes 31485952 | tf_op jit(solution)/shard_map/dot_general | solution.py:212
  477.6 16.3 %fusion.47 = (bf16[4096]{0:T(1024)(128)(2,1)}, bf16[512,4096]{1,0:T(8,128)(2,1)}) fusion(f32[512,4096]{1,0:T(8,128)} %get-tuple-element.179, bf16[4096,1024]{1,0:T(8,128)(2,1)} %all-gather.22.cloned.1.call-done, bf16[1,512,1024]{2,1,0:T(8,128)(2,1)S(1)} %copy-done.7, f32[512,4096]{1,0:T(8,128)} %get-tuple-element.211, f32[4096]{0:T(1024)S(1)} %convert_element_type.220), kind=kOutput, calls=%fused_computation.129 | convolution fusion | flops 4328517632 | bytes 30433280 | tf_op jit(solution)/shard_map/td,fd->tf/dot_general | solution.py:239
  493.9 123.4 %all-gather.24.cloned.1.call-done = bf16[1024,4096]{1,0:T(8,128)(2,1)} async-done(((bf16[256,4096]{1,0:T(8,128)(2,1)}), bf16[1024,4096]{1,0:T(8,128)(2,1)}) %all-gather.24.cloned.1.call-update) | async-done | bytes 8388624 | tf_op jit(solution)/shard_map/all_gather | solution.py:230
  633.4 51.1 %while.31 = (s32[]{:T(128)}, f32[4,512,256]{1,2,0:T(8,128)}, bf16[4,1024,256]{1,2,0:T(8,128)(2,1)}, bf16[4,1024,256]{1,2,0:T(8,128)(2,1)}, bf16[4,1024,256]{1,2,...) while((s32[]{:T(128)}, f32[4,512,256]{1,2,0:T(8,128)}, ...), condition=%wide.region_12.13_spmd.clone, body=%wide.region_10.12_spmd.sunk.clone | while | flops 1361704960 | bytes 73465992 | solution.py:260
  702.1 12.7 reduce-scatter.7.cloned.1.call-done
  720.2 28.7 %reduce-scatter.9.cloned.1.call-done = bf16[4,512,256]{1,2,0:T(8,128)(2,1)} async-done(((bf16[4,1024,256]{1,2,0:T(8,128)(2,1)}), bf16[4,512,256]{1,2,0:T(8,128)(2,1)}) %reduce-scatter.9.cloned.1.call-update) | async-done | bytes 1048592 | tf_op jit(solution)/shard_map/reduce_scatter | solution.py:268
  769.2 11.7 all-gather.6
  783.4 11.5 reduce-scatter.13.cloned.1.call-done
  795.0 146.1 %reduce-scatter.17.cloned.1.call-done = bf16[1024,1024]{1,0:T(8,128)(2,1)} async-done(((bf16[4096,1024]{1,0:T(8,128)(2,1)}), bf16[1024,1024]{1,0:T(8,128)(2,1)}) %reduce-scatter.17.cloned.1.call-update) | async-done | bytes 2097168 | tf_op jit(solution)/shard_map/reduce_scatter | solution.py:339
  941.0 113.7 %reduce-scatter.11.cloned.1.call-done = bf16[256,3072]{1,0:T(8,128)(2,1)} async-done(((bf16[1024,3072]{1,0:T(8,128)(2,1)}), bf16[256,3072]{1,0:T(8,128)(2,1)}) %reduce-scatter.11.cloned.1.call-update) | async-done | bytes 1572880 | tf_op jit(solution)/shard_map/reduce_scatter | solution.py:315
  1054.8 147.4 %reduce-scatter.15.cloned.1.call-done = bf16[256,4096]{1,0:T(8,128)(2,1)} async-done(((bf16[1024,4096]{1,0:T(8,128)(2,1)}), bf16[256,4096]{1,0:T(8,128)(2,1)}) %reduce-scatter.15.cloned.1.call-update) | async-done | bytes 2097168 | tf_op jit(solution)/shard_map/reduce_scatter | solution.py:333
  1202.2 10.3 fusion.24
  1221.7 18.9 %all-reduce.10 = (bf16[1024]{0:T(1024)(128)(2,1)S(1)}, bf16[1024]{0:T(1024)(128)(2,1)S(1)}, bf16[3072]{0:T(1024)(128)(2,1)S(1)}, bf16[1024]{0:T(1024)(128)(2,1)S...) all-reduce(bf16[1024]{0:T(1024)(128)(2,1)S(1)} %get-tuple-element.1, ...), channel_id=4, replica_groups=mesh['rep'=4,'fsdp'=4,'seq'=2] {'fsdp'}, use_global_device_ids=true, to_apply=%region_18.19.clone | all-reduce | flops 13312 | bytes 53248
  1241.1 14.9 %all-reduce.8 = (bf16[256]{0:T(256)(128)(2,1)S(1)}, bf16[256]{0:T(256)(128)(2,1)S(1)}, bf16[768]{0:T(1024)(128)(2,1)S(1)}, bf16[256]{0:T(256)(128)(2,1)S(1)}, bf...) all-reduce(bf16[256]{0:T(256)(128)(2,1)S(1)} %dynamic-slice.1, ...), channel_id=1, replica_groups=mesh['rep'=4,'fsdp'=4,'seq'=2] {'rep','seq'}, use_global_device_ids=true, to_apply=%region_19.20 | all-reduce | flops 3328 | bytes 13312 | tf_op jit(solution)/shard_map/psum | solution.py:347
  1264.7 46.2 %all-reduce.13.cloned.1.call-done = (bf16[256,3072]{1,0:T(8,128)(2,1)}, bf16[256,1024]{1,0:T(8,128)(2,1)}, bf16[256,4096]{1,0:T(8,128)(2,1)}, bf16[1024,1024]{1,0:T(8,128)(2,1)}) async-done(((bf16[256,3072]{1,0:T(8,128)(2,1)}, bf16[256,1024]{1,0:T(8,128)(2,1)}, bf16[256,4096]{1,0:T(8,128)(2,1)}, bf16[1024,1024]{1,0:T(8,128)(2,1)}), (bf16[256,3072]{1,0:T(8,128)(2,1)}, bf16[256,1024]{1,0:T(8,128)(2,1)}, ...) | async-done | bytes 6291472 | tf_op jit(solution)/shard_map/psum | solution.py:349
  (343 shorter events, 236.1 us)
Async XLA Ops:
  7.2 120.6 %all-gather.14.cloned.1.call-start = ((), (), s32[]{:S(2)}) async-start(), calls=%async_computation.6 | async-start | bytes 7864320 | tf_op jit(solution)/shard_map/all_gather | solution.py:151
  7.9 406.0 %all-gather.16.cloned.1.call-start = ((), (), s32[]{:S(2)}) async-start(), calls=%async_computation.7 | async-start | bytes 3145728 | tf_op jit(solution)/shard_map/all_gather | solution.py:201
  36.6 91.2 %copy-start.47 = (f32[4,1,256]{2,1,0:T(1,128)}, f32[4,1,256]{2,1,0:T(1,128)S(1)}, u32[]{:S(2)}) copy-start(f32[4,1,256]{2,1,0:T(1,128)S(1)} %convert_element_type.251) | copy-start | bytes 12292
  138.0 275.9 %all-gather.18.cloned.1.call-start = ((), (), s32[]{:S(2)}) async-start(), calls=%async_computation.8 | async-start | bytes 3145728 | tf_op jit(solution)/shard_map/all_gather | solution.py:200
  155.9 204.8 %copy-start.51 = (bf16[1024]{0:T(1024)(128)(2,1)S(1)}, bf16[1024]{0:T(1024)(128)(2,1)}, u32[]{:S(2)}) copy-start(bf16[1024]{0:T(1024)(128)(2,1)} %param.30) | copy-start | bytes 6148
  155.9 223.6 %copy-start.55 = (bf16[256]{0:T(256)(128)(2,1)S(1)}, bf16[256]{0:T(256)(128)(2,1)}, u32[]{:S(2)}) copy-start(bf16[256]{0:T(256)(128)(2,1)} %param.28) | copy-start | bytes 1540
  155.9 235.0 %copy-start.56 = (bf16[256]{0:T(256)(128)(2,1)S(1)}, bf16[256]{0:T(256)(128)(2,1)}, u32[]{:S(2)}) copy-start(bf16[256]{0:T(256)(128)(2,1)} %param.27) | copy-start | bytes 1540
  157.5 288.2 %all-gather.20.cloned.1.call-start = ((), (), s32[]{:S(2)}) async-start(), calls=%async_computation.9 | async-start | bytes 2621440 | tf_op jit(solution)/shard_map/all_gather | solution.py:153
  158.1 319.5 %all-gather.22.cloned.1.call-start = ((), (), s32[]{:S(2)}) async-start(), calls=%async_computation.10 | async-start | bytes 10485760 | tf_op jit(solution)/shard_map/all_gather | solution.py:159
  158.7 458.6 %all-gather.24.cloned.1.call-start = ((), (), s32[]{:S(2)}) async-start(), calls=%async_computation.11 | async-start | bytes 10485760 | tf_op jit(solution)/shard_map/all_gather | solution.py:230
  158.7 50.7 %collective-permute-start = (bf16[256,4096]{1,0:T(8,128)(2,1)}, bf16[256,4096]{1,0:T(8,128)(2,1)}, u32[]{:S(2)}, u32[]{:S(2)}) collective-permute-start(bf16[256,4096]{1,0:T(8,128)(2,1)} %param.29), channel_id=1, source_target_pairs={{0,2},{2,4},{4,6},{6,0},{1,3},{3,5},{5,7},{7,1},{8,10},{10,12},{12... | collective-permute-start | bytes 6291464 | tf_op jit(solution)/shard_map/ppermute | solution.py:17
  158.8 247.3 %collective-permute-start.1 = (bf16[256,4096]{1,0:T(8,128)(2,1)}, bf16[256,4096]{1,0:T(8,128)(2,1)}, u32[]{:S(2)}, u32[]{:S(2)}) collective-permute-start(bf16[256,4096]{1,0:T(8,128)(2,1)} %param.29), channel_id=1, source_target_pairs={{0,6},{2,0},{4,2},{6,4},{1,7},{3,1},{5,3},{7,5},{8,14},{10,8},{12,... | collective-permute-start | bytes 6291464 | tf_op jit(solution)/shard_map/ppermute | solution.py:20
  209.4 198.6 %collective-permute-start.2 = (bf16[256,4096]{1,0:T(8,128)(2,1)}, bf16[256,4096]{1,0:T(8,128)(2,1)}, u32[]{:S(2)}, u32[]{:S(2)}) collective-permute-start(bf16[256,4096]{1,0:T(8,128)(2,1)} %collective-permute-done), channel_id=1, source_target_pairs={{0,2},{2,4},{4,6},{6,0},{1,3},{3,5},{5,7},{7,1},{8,10},{10,12},{12... | collective-permute-start | bytes 6291464 | tf_op jit(solution)/shard_map/ppermute | solution.py:17
  209.5 505.3 %reduce-scatter.7.cloned.1.call-start = ((), (), s32[]{:S(2)}) async-start(), calls=%async_computation.12 | async-start | bytes 3145728 | tf_op jit(solution)/shard_map/reduce_scatter | solution.py:265
  402.2 224.4 %copy-start.40 = (f32[4,1,256]{2,1,0:T(1,128)}, f32[4,1,256]{2,1,0:T(1,128)S(1)}, u32[]{:S(2)}) copy-start(f32[4,1,256]{2,1,0:T(1,128)S(1)} %convert_element_type.254) | copy-start | bytes 12292
  450.4 176.2 %copy-start.4 = (f32[512,1024]{1,0:T(8,128)}, f32[512,1024]{1,0:T(8,128)S(1)}, u32[]{:S(2)}) copy-start(f32[512,1024]{1,0:T(8,128)S(1)} %get-tuple-element.210) | copy-start | bytes 6291460
  450.4 176.2 %copy-start.38 = (f32[512]{0:T(512)}, f32[512]{0:T(512)S(1)}, u32[]{:S(2)}) copy-start(f32[512]{0:T(512)S(1)} %broadcast_multiply_fusion) | copy-start | bytes 6148
  450.8 175.8 %copy-start.43 = (f32[512]{0:T(512)}, f32[512]{0:T(512)S(1)}, u32[]{:S(2)}) copy-start(f32[512]{0:T(512)S(1)} %fusion.33) | copy-start | bytes 6148
  684.5 64.4 %reduce-scatter.9.cloned.1.call-start = ((), (), s32[]{:S(2)}) async-start(), calls=%async_computation.13 | async-start | bytes 3145728 | tf_op jit(solution)/shard_map/reduce_scatter | solution.py:268
  685.3 109.7 %reduce-scatter.13.cloned.1.call-start = ((), (), s32[]{:S(2)}) async-start(), calls=%async_computation.15 | async-start | bytes 2621440 | tf_op jit(solution)/shard_map/reduce_scatter | solution.py:321
  688.3 252.7 %reduce-scatter.17.cloned.1.call-start = ((), (), s32[]{:S(2)}) async-start(), calls=%async_computation.17 | async-start | bytes 10485760 | tf_op jit(solution)/shard_map/reduce_scatter | solution.py:339
  698.0 356.7 %reduce-scatter.11.cloned.1.call-start = ((), (), s32[]{:S(2)}) async-start(), calls=%async_computation.14 | async-start | bytes 7864320 | tf_op jit(solution)/shard_map/reduce_scatter | solution.py:315
  756.7 445.4 %reduce-scatter.15.cloned.1.call-start = ((), (), s32[]{:S(2)}) async-start(), calls=%async_computation.16 | async-start | bytes 10485760 | tf_op jit(solution)/shard_map/reduce_scatter | solution.py:333
  767.7 543.2 %all-reduce.13.cloned.1.call-start = ((), (), s32[]{:S(2)}) async-start(), calls=%async_computation.18 | async-start | bytes 12582912 | tf_op jit(solution)/shard_map/psum | solution.py:349
  (51 other events, 875.8 us)
Sparse Core Ops, SparseCore 0:
  9.6 118.1 all-gather.13
  138.2 31.2 all-gather.15
  171.6 33.0 all-gather.17
  206.1 75.7 all-gather.19
  283.4 184.4 all-gather.21
  469.3 147.9 all-gather.23
  684.6 30.0 reduce-scatter.6
  717.0 31.8 reduce-scatter.8
  751.2 43.6 reduce-scatter.12
  797.2 143.8 reduce-scatter.16
  943.3 111.3 reduce-scatter.10
  1057.0 145.1 reduce-scatter.14
  1205.7 105.1 all-reduce.12
